TPU v7x, 128 devices: a whole 4x4x4 slice. The times are simulated.
128 devices in a mesh: segment: 8 (over x, core), blk: 16 (over y, z).
Axes of the slice: x: 4, y: 4, z: 4, core: 2. Of those that a mesh axis runs over, the one named last changes fastest.
Arguments:
- fresh: bfloat16 [256, 4096], replicated, may hold values from -6 to 6
- previous: bfloat16 [8, 256, 4096], P('segment'), may hold values from -6 to 6
- span_index: int32 [8], P('segment'), may hold values from 0 to 7
- cache_counts: int32 [8, 16], P('segment'), may hold values from 1 to 2048, 16384 in all within a row
- norm_gain: float32 [8, 4096], P('segment'), may hold values from 0.1 to 1.9
- w_query: bfloat16 [8, 4096, 4096], P('segment', None, 'blk'), may hold values from -0.375 to 0.375
- w_keyval: bfloat16 [8, 4096, 2048], P('segment', None, 'blk'), may hold values from -0.09375 to 0.09375
- w_out: bfloat16 [8, 4096, 4096], P('segment', 'blk'), may hold values from -0.09375 to 0.09375
- cache_keys: bfloat16 [8, 32768, 1024], P('segment', 'blk'), may hold values from -220 to 220
- cache_values: bfloat16 [8, 32768, 1024], P('segment', 'blk'), may hold values from -6 to 6
Outputs:
- mixed: bfloat16 [8, 256, 4096], P('segment')
Inputs may be any that keep to these rules, and one draw needn't show every extreme that they name: Each row of cache_counts sums to 16384 and its largest entry is 2048.
All inputs are finite; a program needn't handle non-finite values.
Results may differ from a plain program's by a relative error of at most 0.012.
Values may be sent and summed in bfloat16 or wider, within the bound.
No kernel may reach another device: no remote copies, remote signals or barrier semaphores. Data moves between devices by JAX's collectives and lax.ppermute only.
A program may use at most 128 MiB of HBM per device.

v0:
```python
import jax
import jax.numpy as jnp
from jax import lax
from jax.sharding import PartitionSpec as P

KVH = 8
HD = 128
ROPE_BASE = 500000.0
EPSILON = 1e-05


def passed_along(block, axis, distance):
    devices = range(lax.axis_size(axis))
    route = [(i - distance, i) for i in devices if i - distance in devices]
    return lax.ppermute(block, axis, route)


def swapped(block, axis, distance):
    count = lax.axis_size(axis)
    route = []
    for low in range(count):
        high = low | 1 << distance
        if high != low and high < count:
            route += [(low, high), (high, low)]
    return lax.ppermute(block, axis, route)


def rotate(projected, first_span):
    length = projected.shape[0]
    half_width = projected.shape[-1] // 2
    positions = (first_span * length + jnp.arange(length, dtype=jnp.int32)).astype(jnp.float32)
    inverse = ROPE_BASE ** (
        -(jnp.arange(half_width, dtype=jnp.float32) * 2.0) / projected.shape[-1]
    )
    angles = positions[:, None] * inverse[None, :]
    cosine = jnp.cos(angles)[:, None, :]
    sine_table = jnp.sin(angles)[:, None, :]
    left_part = projected[..., :half_width]
    right_part = projected[..., half_width:]
    return jnp.concatenate(
        [
            left_part * cosine - right_part * sine_table,
            right_part * cosine + left_part * sine_table,
        ],
        axis=-1,
    )


def attend_rows(query_rows, key_rows, value_rows, allowed):
    scores = lax.dot_general(
        query_rows, key_rows, (((1,), (1,)), ((), ())), preferred_element_type=jnp.float32
    ) * query_rows.shape[-1] ** (-0.5)
    scores = jnp.where(allowed, scores, -jnp.inf)
    highest = jnp.max(scores, axis=-1, keepdims=True)
    weights = jnp.exp(scores - highest)
    totals = jnp.sum(weights, axis=-1, keepdims=True)
    partial_out = (
        jnp.dot(weights.astype(jnp.bfloat16), value_rows, preferred_element_type=jnp.float32)
        / totals
    ).astype(jnp.bfloat16)
    return (partial_out, (highest + jnp.log(totals))[:, 0])


def shards(
    fresh,
    previous,
    span_index,
    cache_counts,
    norm_gain,
    w_query,
    w_keyval,
    w_out,
    cache_keys,
    cache_values,
):
    blocks = lax.axis_size("blk")
    position = lax.axis_index("blk")
    span_rows = fresh.shape[0]
    arrived = passed_along(previous[0], "segment", 1)
    current = jnp.where(lax.axis_index("segment") == 0, fresh, arrived)
    widened = current.astype(jnp.float32)
    normed = (
        widened
        * lax.rsqrt(jnp.mean(widened * widened, axis=-1, keepdims=True) + EPSILON)
        * norm_gain[0]
    ).astype(jnp.bfloat16)
    first_span = span_index[0]
    heads_here = w_query.shape[2] // HD
    ratio = blocks // KVH
    queries = jnp.dot(normed, w_query[0], preferred_element_type=jnp.float32).reshape(
        span_rows, heads_here, HD
    )
    queries = rotate(queries, first_span).astype(jnp.bfloat16).reshape(span_rows, heads_here * HD)
    projected = jnp.dot(normed, w_keyval[0], preferred_element_type=jnp.float32)
    odd_member = position % 2 == 1
    as_key = rotate(projected[:, None, :], first_span)[:, 0, :].astype(jnp.bfloat16)
    mine = jnp.where(odd_member, projected.astype(jnp.bfloat16), as_key)
    partner = swapped(mine, "blk", 0)
    own_keys = jnp.where(odd_member, partner, mine)
    own_values = jnp.where(odd_member, mine, partner)
    query_rows = queries.reshape(span_rows * heads_here, HD)
    row_tokens = jnp.arange(span_rows * heads_here, dtype=jnp.int32) // heads_here
    causal = row_tokens[:, None] >= jnp.arange(span_rows, dtype=jnp.int32)[None, :]
    own_out, own_log = attend_rows(query_rows, own_keys, own_values, causal)
    own_out = own_out.reshape(span_rows, heads_here * HD)
    own_log = own_log.reshape(span_rows, heads_here).T
    cache_rows = cache_keys.shape[1]
    offsets = jnp.arange(cache_rows, dtype=jnp.int32)
    every_query = lax.all_gather(queries, "blk", axis=0, tiled=True)
    live = cache_counts[0, position]

    def holder(source):
        query_block = lax.dynamic_slice_in_dim(
            every_query, source * span_rows, span_rows, 0
        ).reshape(span_rows * heads_here, HD)
        head_start = source // ratio * HD
        key_rows = lax.dynamic_slice_in_dim(cache_keys[0], head_start, HD, 1)
        value_rows = lax.dynamic_slice_in_dim(cache_values[0], head_start, HD, 1)
        partial_out, log_totals = attend_rows(
            query_block, key_rows, value_rows, (offsets < live)[None, :]
        )
        return (
            partial_out.reshape(span_rows, heads_here * HD),
            log_totals.reshape(span_rows, heads_here).T,
        )

    held_outs, held_logs = lax.map(holder, jnp.arange(blocks, dtype=jnp.int32))
    shard_outs = lax.all_to_all(held_outs, "blk", split_axis=0, concat_axis=0, tiled=True)
    shard_logs = lax.all_to_all(held_logs, "blk", split_axis=0, concat_axis=0, tiled=True)
    all_outs = (
        jnp.concatenate([own_out[None], shard_outs], axis=0)
        .astype(jnp.float32)
        .reshape(blocks + 1, span_rows, heads_here, HD)
    )
    all_logs = jnp.concatenate([own_log[None], shard_logs], axis=0).transpose(0, 2, 1)
    ceiling = jnp.max(all_logs, axis=0)
    factors = jnp.exp(all_logs - ceiling)
    attended = (
        jnp.sum(factors[..., None] * all_outs, axis=0) / jnp.sum(factors, axis=0)[..., None]
    ).astype(jnp.bfloat16)
    attended = attended.reshape(span_rows, heads_here * HD)
    head_terms = lax.optimization_barrier(
        jnp.dot(attended, w_out[0], preferred_element_type=jnp.float32).astype(jnp.bfloat16)
    ).astype(jnp.float32)
    summed = lax.psum(head_terms.astype(jnp.bfloat16), "blk").astype(jnp.float32)
    mixed = (widened + summed).astype(jnp.bfloat16)
    return mixed[None]


def solution(mesh):
    placed = (
        P(),
        P("segment", None, None),
        P("segment"),
        P("segment", None),
        P("segment", None),
        P("segment", None, "blk"),
        P("segment", None, "blk"),
        P("segment", "blk", None),
        P("segment", "blk", None),
        P("segment", "blk", None),
    )
    return jax.shard_map(
        shards, mesh=mesh, in_specs=placed, out_specs=P("segment", None, None), check_vma=False
    )
```

profile of v0, /device:TPU:0, one launch (start us, length us, event | category | flops | bytes accessed | tf_op | source)
XLA Modules:
  0.0 425.8 jit_solution(5192613194957220926)
XLA Ops:
  6.5 2.8 collective-permute-start
  9.3 4.1 copy.33
  14.4 2.7 fusion.23
  19.9 67.0 %all-gather.2.cloned.1.call-done = bf16[4096,256]{1,0:T(8,128)(2,1)} async-done(((bf16[256,256]{1,0:T(8,128)(2,1)}), bf16[4096,256]{1,0:T(8,128)(2,1)}) %all-gather.2.cloned.1.call-update) | async-done | bytes 2097168 | tf_op jit(solution)/shard_map/all_gather | solution.py:109
  87.0 177.8 %while.15 = (s32[]{:T(128)}, bf16[16,256,256]{2,1,0:T(8,128)(2,1)}, f32[16,2,256]{2,1,0:T(2,128)S(1)}, s32[]{:T(128)}, s32[16]{0:T(128)S(1)}, /*index=5*/bf16[40...) while((s32[]{:T(128)}, bf16[16,256,256]{2,1,0:T(8,128)(2,1)}, ...), condition=%wide.region_6.7_spmd.clone, body=%wide.region_3.6_spmd.clone.sunk | while | flops 548537856 | bytes 14979499 | solution.py:127
  95.1 2.0 fusion.79
  106.2 2.0 fusion.79
  117.3 2.0 fusion.79
  125.6 1.9 fusion.77
  128.4 2.0 fusion.79
  139.5 2.0 fusion.79
  150.6 2.0 fusion.79
  161.8 2.0 fusion.79
  172.9 2.0 fusion.79
  184.0 2.0 fusion.79
  195.1 2.0 fusion.79
  206.2 2.0 fusion.79
  217.3 2.0 fusion.79
  228.5 2.0 fusion.79
  239.6 2.0 fusion.79
  250.7 2.0 fusion.79
  261.8 2.0 fusion.79
  264.8 12.4 %all_to_all.10 = f32[16,2,256]{2,1,0:T(2,128)S(1)} all-to-all(f32[16,2,256]{2,1,0:T(2,128)S(1)} %get-tuple-element.120), channel_id=1, replica_groups=mesh['segment'=8,'blk'=16] {'blk'}, dimensions={0} | all-to-all | bytes 65536 | tf_op jit(solution)/shard_map/all_to_all | solution.py:129
  277.2 4.4 %all-to-all-start.1 = ((bf16[16,256,256]{2,1,0:T(8,128)(2,1)}), bf16[16,256,256]{2,1,0:T(8,128)(2,1)}, u32[]{:S(2)}, u32[]{:S(2)}) async-start(bf16[16,256,256]{2,1,0:T(8,128)(2,1)} %get-tuple-element.121), calls=%async_computation.1 | async-start | bytes 4194304 | tf_op jit(solution)/shard_map/all_to_all | solution.py:128
  281.6 2.8 fusion.33
  286.9 18.0 %collective-permute-done.1 = bf16[256,128]{0,1:T(8,128)(2,1)S(1)} collective-permute-done((bf16[256,128]{0,1:T(8,128)(2,1)S(1)}, bf16[256,128]{0,1:T(8,128)(2,1)S(1)}, u32[]{:S(2)}, u32[]{:S(2)}) %collective-permute-start.1) | collective-permute-done | bytes 65568 | tf_op jit(solution)/shard_map/ppermute | solution.py:25
  306.0 2.1 copy.31
  309.4 4.0 concatenate.34
  313.4 7.7 %multiply_reduce_fusion = f32[256,2,128]{2,1,0:T(2,128)S(1)} fusion(bf16[16,256,2,128]{3,2,1,0:T(2,128)(2,1)} %concatenate.34, bf16[1,256,2,128]{3,2,1,0:T(2,128)(2,1)S(1)} %bitcast.73, f32[17,256,2]{2,1,0:T(8,128)} %copy.31), kind=kLoop, calls=%fused_computation.28 | loop fusion | flops 4390912 | bytes 2525184 | tf_op jit(solution)/shard_map/reduce_sum | solution.py:139
  321.5 2.0 convolution_convert_fusion
  323.5 91.1 %all-reduce.2.cloned.1.call-done = bf16[256,4096]{1,0:T(8,128)(2,1)} async-done(((bf16[256,4096]{1,0:T(8,128)(2,1)}), bf16[256,4096]{1,0:T(8,128)(2,1)}) %all-reduce.2.cloned.1.call-update) | async-done | bytes 2097168 | tf_op jit(solution)/shard_map/psum | solution.py:145
  414.6 4.3 %fusion.27 = bf16[1,256,4096]{2,1,0:T(8,128)(2,1)} fusion(bf16[256,4096]{1,0:T(8,128)(2,1)} %all-reduce.2.cloned.1.call-done, bf16[256,4096]{1,0:T(8,128)(2,1)} %copy-done.1), kind=kLoop, calls=%fused_computation.33 | loop fusion | flops 4194304 | bytes 6291456 | tf_op jit(solution)/shard_map/broadcast_in_dim | solution.py:147
  (235 shorter events, 101.5 us)
Async XLA Ops:
  6.5 314.9 %copy-start = (bf16[1,256,4096]{2,1,0:T(8,128)(2,1)S(1)}, bf16[1,256,4096]{2,1,0:T(8,128)(2,1)}, u32[]{:S(2)}) copy-start(bf16[1,256,4096]{2,1,0:T(8,128)(2,1)} %param.19) | copy-start | bytes 6291460
  6.5 80.4 %all-gather.2.cloned.1.call-start = ((), (), s32[]{:S(2)}) async-start(), calls=%async_computation.2 | async-start | bytes 2228224 | tf_op jit(solution)/shard_map/all_gather | solution.py:109
  6.5 7.9 %collective-permute-start = (bf16[256,4096]{1,0:T(8,128)(2,1)}, bf16[256,4096]{1,0:T(8,128)(2,1)}, u32[]{:S(2)}, u32[]{:S(2)}) collective-permute-start(bf16[256,4096]{1,0:T(8,128)(2,1)} %bitcast.76), channel_id=1, source_target_pairs={{0,16},{16,32},{32,48},{48,64},{64,80},{80,96},{96,112},{1,17},{17... | collective-permute-start | bytes 6291464 | tf_op jit(solution)/shard_map/ppermute | solution.py:15
  14.4 2.8 copy-start.2
  14.4 2.8 copy-start.3
  17.1 1.3 copy-start.1
  17.2 2.1 copy-start.4
  277.2 32.3 %all-to-all-start.1 = ((bf16[16,256,256]{2,1,0:T(8,128)(2,1)}), bf16[16,256,256]{2,1,0:T(8,128)(2,1)}, u32[]{:S(2)}, u32[]{:S(2)}) async-start(bf16[16,256,256]{2,1,0:T(8,128)(2,1)} %get-tuple-element.121), calls=%async_computation.1 | async-start | bytes 4194304 | tf_op jit(solution)/shard_map/all_to_all | solution.py:128
  281.6 133.0 %all-reduce.2.cloned.1.call-start = ((), (), s32[]{:S(2)}) async-start(), calls=%async_computation.3 | async-start | bytes 4194304 | tf_op jit(solution)/shard_map/psum | solution.py:145
  284.8 20.1 %collective-permute-start.1 = (bf16[256,128]{0,1:T(8,128)(2,1)S(1)}, bf16[256,128]{0,1:T(8,128)(2,1)S(1)}, u32[]{:S(2)}, u32[]{:S(2)}) collective-permute-start(bf16[256,128]{0,1:T(8,128)(2,1)S(1)} %fusion.54), channel_id=1, source_target_pairs={{0,1},{1,0},{2,3},{3,2},{4,5},{5,4},{6,7},{7,6},{8,9},{9,8},{10,11... | collective-permute-start | bytes 196616 | tf_op jit(solution)/shard_map/ppermute | solution.py:25
Sparse Core Ops, SparseCore 0:
  19.4 67.5 all-gather.1
  323.6 90.9 all-reduce.1
where the time goes:
time: 429 us; the launch traced here: 426 us
  waiting for transfers between devices  177 us (41%)
  matrix products  68.5 us (16%)
  local copies, waits for them, and re-layouts  52.7 us (12%)
  loops' own time  50.4 us (12%)
  other arithmetic  41.1 us (10%)
  between operations  14.3 us (3%)
  blocking collectives  12.4 us (3%)
  starting transfers between devices  9.06 us (2%)
    psum x1, waiting for transfers between devices, shards(): lax.psum(head_terms.astype(jnp.bfloat16), 'blk').astype(jnp.float32)  91.1 us
    all_gather x1, waiting for transfers between devices, shards(): every_query = lax.all_gather(queries, 'blk', axis=0, tiled=True)  67 us
    another operation x1, loops' own time, shards(): held_outs, held_logs = lax.map(holder, jnp.arange(blocks, dtype=jnp.int32))  50.4 us
    dot_general x17, matrix products, attend_rows(): jnp.dot(weights.astype(jnp.bfloat16), value_rows, preferred_element_type=...  32.6 us
    dot_general x17, matrix products, attend_rows(): lax.dot_general(query_rows, key_rows, (((1,), (1,)), ((), ())), preferred...  30.1 us
    ppermute x1, waiting for transfers between devices, swapped(): return lax.ppermute(block, axis, route)  18 us
    reduce_sum x17, other arithmetic, attend_rows(): totals = jnp.sum(weights, axis=-1, keepdims=True)  15.2 us
    dynamic_slice x16, local copies, waits for them, and re-layouts, holder(): lax.dynamic_slice_in_dim(every_query, source * span_rows, span_rows, 0)  14.7 us
  transfers between devices with their start and end apart: 5, of which 4 were waited for; matrix products, arithmetic and copies ran while one was open for 3% of the time, Pallas kernels for 0%

commit v1 on v0

--- a/solution.py
+++ b/solution.py
@@ -106,7 +106,9 @@
     own_log = own_log.reshape(span_rows, heads_here).T
     cache_rows = cache_keys.shape[1]
     offsets = jnp.arange(cache_rows, dtype=jnp.int32)
-    every_query = lax.all_gather(queries, "blk", axis=0, tiled=True)
+    every_query = jnp.concatenate(
+        lax.all_to_all(jnp.stack([queries] * lax.axis_size("blk")), "blk", 0, 0), axis=0
+    )
     live = cache_counts[0, position]
 
     def holder(source):

time: 429 us -> 415 us (0.967)
  waiting for transfers between devices: 177 us -> 155 us
  starting transfers between devices: 9.06 us -> 18 us
    all_gather x1 -> x0, waiting for transfers between devices: 67 us -> none  [shards(): every_query = lax.all_gather(queries, 'blk', axis=0, tiled=True)]
    psum x1, waiting for transfers between devices: 91.1 us -> 125 us  [shards(): lax.psum(head_terms.astype(jnp.bfloat16), 'blk').astype(jnp.float32)]
    all_to_all x0 -> x1, waiting for transfers between devices: none -> 18.9 us  [shards(): lax.all_to_all(jnp.stack([queries] * lax.axis_size('blk')), 'blk', 0, 0)]
    all_to_all x0 -> x1, starting transfers between devices: none -> 8.76 us  [shards(): lax.all_to_all(jnp.stack([queries] * lax.axis_size('blk')), 'blk', 0, 0)]
    ppermute x1, waiting for transfers between devices: 18 us -> 9.47 us  [swapped(): return lax.ppermute(block, axis, route)]
where the time goes in v1:
time: 415 us; the launch traced here: 412 us
  waiting for transfers between devices  155 us (37%)
  matrix products  68.5 us (17%)
  local copies, waits for them, and re-layouts  53.5 us (13%)
  loops' own time  50.5 us (12%)
  other arithmetic  41.1 us (10%)
  starting transfers between devices  18 us (4%)
  between operations  14.3 us (3%)
  blocking collectives  11.3 us (3%)
    psum x1, waiting for transfers between devices, shards(): lax.psum(head_terms.astype(jnp.bfloat16), 'blk').astype(jnp.float32)  125 us
    another operation x1, loops' own time, shards(): held_outs, held_logs = lax.map(holder, jnp.arange(blocks, dtype=jnp.int32))  50.5 us
    dot_general x17, matrix products, attend_rows(): jnp.dot(weights.astype(jnp.bfloat16), value_rows, preferred_element_type=...  32.6 us
    dot_general x17, matrix products, attend_rows(): lax.dot_general(query_rows, key_rows, (((1,), (1,)), ((), ())), preferred...  30.2 us
    all_to_all x1, waiting for transfers between devices, shards(): lax.all_to_all(jnp.stack([queries] * lax.axis_size('blk')), 'blk', 0, 0)  18.9 us
    reduce_sum x17, other arithmetic, attend_rows(): totals = jnp.sum(weights, axis=-1, keepdims=True)  15.2 us
    dynamic_slice x16, local copies, waits for them, and re-layouts, holder(): lax.dynamic_slice_in_dim(every_query, source * span_rows, span_rows, 0)  14.7 us
    dynamic_update_slice x48, local copies, waits for them, and re-layouts, shards(): held_outs, held_logs = lax.map(holder, jnp.arange(blocks, dtype=jnp.int32))  12.2 us
  transfers between devices with their start and end apart: 5, of which 4 were waited for; matrix products, arithmetic and copies ran while one was open for 3% of the time, Pallas kernels for 0%

profile of v1, /device:TPU:0, one launch (start us, length us, event | category | flops | bytes accessed | tf_op | source)
XLA Modules:
  0.0 412.0 jit_solution(13070000664983280524)
XLA Ops:
  6.5 2.8 collective-permute-start
  10.0 4.1 copy.33
  14.4 2.7 fusion.23
  20.1 8.8 %all-to-all-start = ((bf16[16,256,256]{2,1,0:T(8,128)(2,1)}), bf16[16,256,256]{2,1,0:T(8,128)(2,1)}, u32[]{:S(2)}, u32[]{:S(2)}) async-start(bf16[16,256,256]{2,1,0:T(8,128)(2,1)} %stack.3), calls=%async_computation | async-start | bytes 4194304 | tf_op jit(solution)/shard_map/all_to_all | solution.py:110
  29.5 18.9 %all-to-all-done = bf16[16,256,256]{2,1,0:T(8,128)(2,1)} async-done(((bf16[16,256,256]{2,1,0:T(8,128)(2,1)}), bf16[16,256,256]{2,1,0:T(8,128)(2,1)}, u32[]{:S(2)}, u32[]{:S(2)}) %all-to-all-start) | async-done | bytes 2097184 | tf_op jit(solution)/shard_map/all_to_all | solution.py:110
  48.4 177.9 %while.15 = (s32[]{:T(128)}, bf16[16,256,256]{2,1,0:T(8,128)(2,1)}, f32[16,2,256]{2,1,0:T(2,128)S(1)}, s32[]{:T(128)}, s32[16]{0:T(128)S(1)}, /*index=5*/bf16[40...) while((s32[]{:T(128)}, bf16[16,256,256]{2,1,0:T(8,128)(2,1)}, ...), condition=%wide.region_6.7_spmd.clone, body=%wide.region_3.6_spmd.clone.sunk | while | flops 548537856 | bytes 14979499 | solution.py:129
  56.5 2.0 fusion.79
  67.6 2.0 fusion.79
  78.7 2.0 fusion.79
  89.8 2.0 fusion.79
  101.0 2.0 fusion.79
  112.1 2.0 fusion.79
  123.2 2.0 fusion.79
  134.3 2.0 fusion.79
  145.4 2.0 fusion.79
  156.5 2.0 fusion.79
  167.7 2.0 fusion.79
  178.8 2.0 fusion.79
  189.9 2.0 fusion.79
  201.0 2.0 fusion.79
  212.1 2.0 fusion.79
  223.2 2.0 fusion.79
  226.2 11.3 %all_to_all.15 = f32[16,2,256]{2,1,0:T(2,128)S(1)} all-to-all(f32[16,2,256]{2,1,0:T(2,128)S(1)} %get-tuple-element.120), channel_id=1, replica_groups=mesh['segment'=8,'blk'=16] {'blk'}, dimensions={0} | all-to-all | bytes 65536 | tf_op jit(solution)/shard_map/all_to_all | solution.py:131
  237.5 4.4 %all-to-all-start.2 = ((bf16[16,256,256]{2,1,0:T(8,128)(2,1)}), bf16[16,256,256]{2,1,0:T(8,128)(2,1)}, u32[]{:S(2)}, u32[]{:S(2)}) async-start(bf16[16,256,256]{2,1,0:T(8,128)(2,1)} %get-tuple-element.121), calls=%async_computation.2 | async-start | bytes 4194304 | tf_op jit(solution)/shard_map/all_to_all | solution.py:130
  242.0 2.8 fusion.33
  247.4 9.5 %collective-permute-done.1 = bf16[256,128]{0,1:T(8,128)(2,1)S(1)} collective-permute-done((bf16[256,128]{0,1:T(8,128)(2,1)S(1)}, bf16[256,128]{0,1:T(8,128)(2,1)S(1)}, u32[]{:S(2)}, u32[]{:S(2)}) %collective-permute-start.1) | collective-permute-done | bytes 65568 | tf_op jit(solution)/shard_map/ppermute | solution.py:25
  258.1 2.1 copy.31
  261.5 4.0 concatenate.34
  265.5 7.7 %multiply_reduce_fusion = f32[256,2,128]{2,1,0:T(2,128)S(1)} fusion(bf16[16,256,2,128]{3,2,1,0:T(2,128)(2,1)} %concatenate.34, bf16[1,256,2,128]{3,2,1,0:T(2,128)(2,1)S(1)} %bitcast.74, f32[17,256,2]{2,1,0:T(8,128)} %copy.31), kind=kLoop, calls=%fused_computation.28 | loop fusion | flops 4390912 | bytes 2525184 | tf_op jit(solution)/shard_map/reduce_sum | solution.py:141
  273.6 2.0 convolution_convert_fusion
  275.6 125.2 %all-reduce.2.cloned.1.call-done = bf16[256,4096]{1,0:T(8,128)(2,1)} async-done(((bf16[256,4096]{1,0:T(8,128)(2,1)}), bf16[256,4096]{1,0:T(8,128)(2,1)}) %all-reduce.2.cloned.1.call-update) | async-done | bytes 2097168 | tf_op jit(solution)/shard_map/psum | solution.py:147
  400.8 4.3 %fusion.27 = bf16[1,256,4096]{2,1,0:T(8,128)(2,1)} fusion(bf16[256,4096]{1,0:T(8,128)(2,1)} %all-reduce.2.cloned.1.call-done, bf16[256,4096]{1,0:T(8,128)(2,1)} %copy-done.1), kind=kLoop, calls=%fused_computation.33 | loop fusion | flops 4194304 | bytes 6291456 | tf_op jit(solution)/shard_map/broadcast_in_dim | solution.py:149
  (235 shorter events, 104.4 us)
Async XLA Ops:
  6.5 267.0 %copy-start = (bf16[1,256,4096]{2,1,0:T(8,128)(2,1)S(1)}, bf16[1,256,4096]{2,1,0:T(8,128)(2,1)}, u32[]{:S(2)}) copy-start(bf16[1,256,4096]{2,1,0:T(8,128)(2,1)} %param.19) | copy-start | bytes 6291460
  6.5 7.9 %collective-permute-start = (bf16[256,4096]{1,0:T(8,128)(2,1)}, bf16[256,4096]{1,0:T(8,128)(2,1)}, u32[]{:S(2)}, u32[]{:S(2)}) collective-permute-start(bf16[256,4096]{1,0:T(8,128)(2,1)} %bitcast.77), channel_id=1, source_target_pairs={{0,16},{16,32},{32,48},{48,64},{64,80},{80,96},{96,112},{1,17},{17... | collective-permute-start | bytes 6291464 | tf_op jit(solution)/shard_map/ppermute | solution.py:15
  14.4 2.8 copy-start.2
  14.4 2.8 copy-start.3
  17.1 1.3 copy-start.1
  20.1 8.8 %copy-start.4 = (s32[1,16]{1,0:T(1,128)S(1)}, s32[1,16]{1,0:T(1,128)}, u32[]{:S(2)}) copy-start(s32[1,16]{1,0:T(1,128)} %param.15) | copy-start | bytes 196
  20.1 28.3 %all-to-all-start = ((bf16[16,256,256]{2,1,0:T(8,128)(2,1)}), bf16[16,256,256]{2,1,0:T(8,128)(2,1)}, u32[]{:S(2)}, u32[]{:S(2)}) async-start(bf16[16,256,256]{2,1,0:T(8,128)(2,1)} %stack.3), calls=%async_computation | async-start | bytes 4194304 | tf_op jit(solution)/shard_map/all_to_all | solution.py:110
  237.5 24.0 %all-to-all-start.2 = ((bf16[16,256,256]{2,1,0:T(8,128)(2,1)}), bf16[16,256,256]{2,1,0:T(8,128)(2,1)}, u32[]{:S(2)}, u32[]{:S(2)}) async-start(bf16[16,256,256]{2,1,0:T(8,128)(2,1)} %get-tuple-element.121), calls=%async_computation.2 | async-start | bytes 4194304 | tf_op jit(solution)/shard_map/all_to_all | solution.py:130
  241.9 158.9 %all-reduce.2.cloned.1.call-start = ((), (), s32[]{:S(2)}) async-start(), calls=%async_computation.3 | async-start | bytes 4194304 | tf_op jit(solution)/shard_map/psum | solution.py:147
  245.2 11.7 %collective-permute-start.1 = (bf16[256,128]{0,1:T(8,128)(2,1)S(1)}, bf16[256,128]{0,1:T(8,128)(2,1)S(1)}, u32[]{:S(2)}, u32[]{:S(2)}) collective-permute-start(bf16[256,128]{0,1:T(8,128)(2,1)S(1)} %fusion.54), channel_id=1, source_target_pairs={{0,1},{1,0},{2,3},{3,2},{4,5},{5,4},{6,7},{7,6},{8,9},{9,8},{10,11... | collective-permute-start | bytes 196616 | tf_op jit(solution)/shard_map/ppermute | solution.py:25
Sparse Core Ops, SparseCore 0:
  275.8 124.9 all-reduce.1
